TPU v7x, 256 devices: a whole 4x4x8 slice. The times are simulated.
256 devices in a mesh: req: 64 (over z, x, core), tp: 4 (over y).
Axes of the slice: x: 4, y: 4, z: 8, core: 2. Of those that a mesh axis runs over, the one named last changes fastest.
Arguments:
- hidden: bfloat16 [16384, 2048], P('req'), may hold values from -10.5 to 10.5
- lengths: int32 [64], replicated, may hold values from 1 to 1024, 16384 in all
- dealing: int32 [64], replicated, may hold values from 0 to 63, each once
- norm_gain: bfloat16 [2048], replicated, may hold values from 0.5 to 1.5
- w_query: bfloat16 [2048, 2048], P(None, 'tp'), may hold values from -0.125 to 0.125
- w_key: bfloat16 [2048, 1024], P(None, 'tp'), may hold values from -0.125 to 0.125
- w_value: bfloat16 [2048, 1024], P(None, 'tp'), may hold values from -0.125 to 0.125
- query_gain: bfloat16 [128], replicated, may hold values from 0.5 to 8
- key_gain: bfloat16 [128], replicated, may hold values from 0.5 to 8
- w_out: bfloat16 [2048, 2048], P(None, 'tp'), may hold values from -0.125 to 0.125
Outputs:
- hidden_out: bfloat16 [16384, 2048], P('req', 'tp')
- kv_cache: bfloat16 [2, 64, 1024, 1024], P(None, 'req', None, 'tp')
Inputs may be any that keep to these rules, and one draw needn't show every extreme that they name: The lengths sum to 16384; the largest is exactly 1024. A permutation: dealt slot j, on device j of req, holds prompt dealing[j].
All inputs are finite; a program needn't handle non-finite values.
Results may differ from a plain program's by a relative error of at most 0.012.
The roundings to bfloat16 on the way count: a program that leaves them out, or rounds other values in their place, can miss the bound.
Values may be sent and summed in bfloat16 or wider, within the bound.
No kernel may reach another device: no remote copies, remote signals or barrier semaphores. Data moves between devices by JAX's collectives and lax.ppermute only.
A program may use at most 128 MiB of HBM per device.

v0:
```python
import jax
import jax.numpy as jnp
from jax import lax
from jax.sharding import PartitionSpec as P

EPS = 1e-06
THETA = 1000000.0


def rms_rows(values, scale_gain):
    inv_rms = lax.rsqrt(jnp.mean(values * values, axis=-1, keepdims=True) + EPS)
    return values * inv_rms * scale_gain


def rotate(values, positions):
    features = values.shape[-1]
    half_width = features // 2
    frequency = THETA ** (-(jnp.arange(half_width).astype(jnp.float32) * 2.0) / features)
    angles = positions.astype(jnp.float32)[:, None] * frequency[None, :]
    cosine = jnp.cos(angles)[:, None, :]
    sine_part = jnp.sin(angles)[:, None, :]
    first_half = values[..., :half_width]
    second_half = values[..., half_width:]
    return jnp.concatenate(
        [
            first_half * cosine - second_half * sine_part,
            second_half * cosine + first_half * sine_part,
        ],
        axis=-1,
    )


def project(normed, w_query, w_key, w_value, query_gain, key_gain, positions):
    head_dim = query_gain.shape[0]
    row_count = normed.shape[0]
    query_rows = jnp.dot(normed, w_query, preferred_element_type=jnp.float32).reshape(
        row_count, -1, head_dim
    )
    key_rows = jnp.dot(normed, w_key, preferred_element_type=jnp.float32).reshape(
        row_count, -1, head_dim
    )
    value_rows = jnp.dot(normed, w_value, preferred_element_type=jnp.float32).astype(jnp.bfloat16)
    query_rows = rotate(rms_rows(query_rows, query_gain.astype(jnp.float32)), positions).astype(
        jnp.bfloat16
    )
    key_rows = rotate(rms_rows(key_rows, key_gain.astype(jnp.float32)), positions).astype(
        jnp.bfloat16
    )
    return (query_rows.reshape(row_count, -1), key_rows.reshape(row_count, -1), value_rows)


def attend(query_slot, key_slot, value_slot, prompt_length, head_dim):
    slot_len, query_width = query_slot.shape
    kv_heads = key_slot.shape[1] // head_dim
    group_size = query_width // head_dim // kv_heads
    queries = query_slot.reshape(slot_len, kv_heads, group_size, head_dim)
    keys_split = key_slot.reshape(slot_len, kv_heads, head_dim)
    values_split = value_slot.reshape(slot_len, kv_heads, head_dim)
    scores = jnp.einsum(
        "qkgd,skd->kgqs", queries, keys_split, preferred_element_type=jnp.float32
    ) * head_dim ** (-0.5)
    offsets = jnp.arange(slot_len, dtype=jnp.int32)
    allowed = (offsets[None, :] <= offsets[:, None]) & (offsets[None, :] < prompt_length)
    scores = jnp.where(allowed[None, None], scores, -jnp.inf)
    row_max = jnp.max(scores, axis=-1, keepdims=True)
    weights = jnp.exp(scores - row_max)
    weights = (weights / jnp.sum(weights, axis=-1, keepdims=True)).astype(jnp.bfloat16)
    mixture = jnp.einsum(
        "kgqs,skd->qkgd", weights, values_split, preferred_element_type=jnp.float32
    )
    return mixture.astype(jnp.bfloat16).reshape(slot_len, query_width)


def on_device(
    hidden, lengths, dealing, norm_gain, w_query, w_key, w_value, query_gain, key_gain, w_out
):
    devices = lax.axis_size("req")
    home_index = lax.axis_index("req")
    slice_index = lax.axis_index("tp")
    tok_rows, features = hidden.shape
    head_dim = query_gain.shape[0]
    out_width = w_out.shape[1]
    slot_len = 4 * tok_rows
    capacity = slot_len // devices
    prompt_total = lengths.shape[0]
    prompt_ids = jnp.arange(prompt_total, dtype=jnp.int32)
    prompt_ends = jnp.cumsum(lengths)
    starts = prompt_ends - lengths
    packed_ids = jnp.arange(tok_rows, dtype=jnp.int32) * devices + home_index
    segment = jnp.sum((packed_ids[:, None] >= prompt_ends[None, :]).astype(jnp.int32), axis=1)
    seg_onehot = (segment[:, None] == prompt_ids[None, :]).astype(jnp.int32)
    positions = packed_ids - jnp.sum(seg_onehot * starts[None, :], axis=1)
    inverse = jnp.zeros((prompt_total,), jnp.int32).at[dealing].set(prompt_ids)
    deal_hot = (dealing[:, None] == prompt_ids[None, :]).astype(jnp.int32)
    dealt_starts = jnp.sum(deal_hot * starts[None, :], axis=1)
    dealt_lengths = jnp.sum(deal_hot * lengths[None, :], axis=1)
    first_offset = jnp.mod(home_index - dealt_starts, devices)
    ranks = jnp.arange(capacity, dtype=jnp.int32)
    slot_offset = first_offset[None, :] + ranks[:, None] * devices
    send_valid = slot_offset < dealt_lengths[None, :]
    send_rows = jnp.where(
        send_valid, (dealt_starts[None, :] + slot_offset - home_index) // devices, 0
    ).reshape(-1)
    my_start = lax.dynamic_index_in_dim(dealt_starts, home_index, 0, keepdims=False)
    my_length = lax.dynamic_index_in_dim(dealt_lengths, home_index, 0, keepdims=False)
    roll_shift = jnp.mod(my_start, devices)
    my_slots = jnp.sum(seg_onehot * inverse[None, :], axis=1)
    back_rows = positions // devices * devices + my_slots
    offsets = jnp.arange(slot_len, dtype=jnp.int32)
    gain_values = norm_gain.astype(jnp.float32)
    picked = jnp.take(hidden, send_rows, axis=0).reshape(capacity, devices, hidden.shape[1])
    arrived = lax.all_to_all(
        jnp.where(send_valid[:, :, None], picked, jnp.zeros((), hidden.dtype)),
        "req",
        split_axis=1,
        concat_axis=1,
        tiled=True,
    )
    slot_hidden = jnp.roll(arrived, -roll_shift, axis=1).reshape(slot_len, arrived.shape[2])
    normed = rms_rows(slot_hidden.astype(jnp.float32), gain_values).astype(jnp.bfloat16)
    query_slot, key_slot, value_slot = project(
        normed, w_query, w_key, w_value, query_gain, key_gain, offsets
    )
    mixture = attend(query_slot, key_slot, value_slot, my_length, head_dim)
    sendback = jnp.roll(mixture.reshape(capacity, devices, mixture.shape[1]), roll_shift, axis=1)
    returned = lax.all_to_all(sendback, "req", split_axis=1, concat_axis=1, tiled=True)
    attended = jnp.take(returned.reshape(capacity * devices, -1), back_rows, axis=0)
    kv_cache = jnp.stack([key_slot, value_slot])[:, None]
    summed = jnp.dot(
        lax.all_gather(attended, "tp", axis=1, tiled=True),
        w_out,
        preferred_element_type=jnp.float32,
    )
    branch = lax.optimization_barrier(summed.astype(jnp.bfloat16))
    residual = lax.dynamic_slice_in_dim(hidden, slice_index * out_width, out_width, 1)
    hidden_out = (residual.astype(jnp.float32) + branch.astype(jnp.float32)).astype(jnp.bfloat16)
    return (hidden_out, kv_cache)


def solution(mesh):
    in_specs = (
        P("req", None),
        P(),
        P(),
        P(),
        P(None, "tp"),
        P(None, "tp"),
        P(None, "tp"),
        P(),
        P(),
        P(None, "tp"),
    )
    out_specs = (P("req", "tp"), P(None, "req", None, "tp"))
    return jax.shard_map(
        on_device, mesh=mesh, in_specs=in_specs, out_specs=out_specs, check_vma=False
    )
```

profile of v0, /device:TPU:2, one launch (start us, length us, event | category | flops | bytes accessed | tf_op | source)
XLA Modules:
  0.0 272.4 jit_solution(343829114084428690)
XLA Ops:
  7.2 0.0 copy-start
  7.2 0.9 copy.58
  8.1 0.1 reduce-window.8
  8.2 0.1 reduce.1
  8.3 0.7 sub.85
  9.0 0.8 select_reduce_fusion.2
  9.8 0.7 compare_select_fusion.7
  10.5 0.1 fusion.24
  10.6 0.1 compare_and_fusion
  10.7 0.1 lt.124
  10.7 0.1 copy.59
  10.8 0.1 sub.93
  11.0 0.1 copy.60
  11.1 10.2 %gather_fusion = bf16[1024,2048]{1,0:T(8,128)(2,1)} fusion(bf16[256,2048]{1,0:T(8,128)(2,1)} %param.10, s32[1024]{0:T(1024)S(1)} %broadcast_clamp_fusion), kind=kCustom, calls=%fused_computation | custom fusion | bytes 8392704 | tf_op jit(solution)/shard_map/jit(_take)/gather | solution.py:111
  21.3 9.6 %fusion.10 = bf16[16,64,2048]{2,0,1:T(8,128)(2,1)} fusion(bf16[16,64,2048]{2,1,0:T(8,128)(2,1)} %bitcast.70, pred[16,64]{0,1:T(8,128)(4,1)S(1)} %copy.60, pred[16,64]{0,1:T(8,128)(4,1)S(1)} %copy.59), kind=kLoop, calls=%fused_computation.22 | loop fusion | flops 4194304 | bytes 8390656 | tf_op jit(solution)/shard_map/jit(_where)/select_n | solution.py:113
  30.9 12.3 %all-to-all-start = ((bf16[16,64,2048]{2,0,1:T(8,128)(2,1)}), bf16[16,64,2048]{2,0,1:T(8,128)(2,1)}, u32[]{:S(2)}, u32[]{:S(2)}) async-start(bf16[16,64,2048]{2,0,1:T(8,128)(2,1)} %fusion.10), calls=%async_computation | async-start | bytes 8388608 | tf_op jit(solution)/shard_map/all_to_all | solution.py:112
  43.2 0.0 copy-start.6
  43.3 0.6 dynamic_slice.19
  45.8 0.6 dynamic_slice.21
  46.4 4.0 %copy.80 = bf16[512,2048]{1,0:T(8,128)(2,1)} copy(bf16[512,2048]{0,1:T(8,128)(2,1)} %bitcast.76) | data formatting | bytes 4194304 | tf_op jit(solution)/shard_map/dot_general | solution.py:36
  50.4 1.4 copy.77
  51.9 0.7 iota_compare_fusion.3
  52.5 1.0 multiply_cosine_fusion
  53.5 1.3 fusion.11
  54.9 84.4 %all-to-all-done = bf16[16,64,2048]{2,0,1:T(8,128)(2,1)} async-done(((bf16[16,64,2048]{2,0,1:T(8,128)(2,1)}), bf16[16,64,2048]{2,0,1:T(8,128)(2,1)}, u32[]{:S(2)}, u32[]{:S(2)}) %all-to-all-start) | async-done | bytes 4194336 | tf_op jit(solution)/shard_map/all_to_all | solution.py:112
  139.3 4.5 %copy.62 = bf16[16,64,2048]{2,1,0:T(8,128)(2,1)S(1)} copy(bf16[16,64,2048]{2,0,1:T(8,128)(2,1)} %all-to-all-done) | data formatting | bytes 8388608 | tf_op jit(solution)/shard_map/all_to_all | solution.py:112
  143.8 6.5 %multiply_reduce_fusion = (f32[16,64]{1,0:T(8,128)S(1)}, f32[16,64,2048]{2,1,0:T(8,128)}) fusion(s32[]{:T(128)S(6)} %select_n.166, bf16[16,64,2048]{2,1,0:T(8,128)(2,1)S(1)} %copy.62), kind=kLoop, calls=%fused_computation.16 | loop fusion | flops 12581888 | bytes 12587012 | tf_op jit(solution)/shard_map/reduce_sum | solution.py:11
  150.3 0.1 rsqrt.29
  150.3 4.3 %multiply_convert_fusion = bf16[16,64,2048]{2,1,0:T(8,128)(2,1)S(1)} fusion(f32[16,64,2048]{2,1,0:T(8,128)} %get-tuple-element.17, f32[2048]{0:T(1024)S(1)} %convert_element_type.122, f32[16,64]{1,0:T(8,128)S(1)} %add_rsqrt_fusion.2), kind=kLoop, calls=%fused_computation.15 | loop fusion | flops 6291456 | bytes 12595200 | tf_op jit(solution)/shard_map/convert_element_type | solution.py:120
  154.6 1.5 copy-done.1
  156.1 2.7 fusion.3
  158.8 0.7 copy-done.3
  159.5 2.4 multiply_reduce_fusion.1
  162.0 0.5 multiply_multiply_fusion
  162.4 1.2 subtract_convert_fusion
  163.6 2.4 copy.67
  166.0 1.4 copy.66
  167.4 3.9 %multiply_reduce_fusion.2 = (f32[1024,2]{0,1:T(2,128)S(1)}, f32[1024,2,128]{0,2,1:T(8,128)S(1)}) fusion(bf16[1024,2048,1]{1,0,2:T(8,128)(2,1)} %bitcast.73, bf16[2,128,2048]{2,1,0:T(8,128)(2,1)} %bitcast.80), kind=kOutput, calls=%fused_computation.41 | convolution fusion | flops 1074264064 | bytes 6299648 | tf_op jit(solution)/shard_map/dot_general | solution.py:39
  171.3 0.2 multiply_multiply_fusion.1
  171.5 0.9 multiply_subtract_fusion
  172.4 1.2 copy-done.2
  173.6 2.1 convolution_convert_fusion
  175.7 11.5 %fusion.38 = (f32[2,2,1024]{2,1,0:T(2,128)S(1)}, f32[2,2,1024,1024]{2,3,1,0:T(8,128)}) fusion(pred[1024,1024]{0,1:T(8,128)(4,1)S(1)} %copy-done.5, bf16[1024,2,2,64]{3,0,2,1:T(8,128)(2,1)} %copy.67, bf16[1024,2,2,64]{3,0,2,1:T(8,128)(2,1)} %copy.66, bf16[1024,2,64]{0,2,1:T(8,128)(2,1)} %get-tuple-element.21, bf16[1024,2,64]{0,2,1:T(8,128)(2,1)S(1)} %get-tuple-element.20), kind=kOutput, calls=%fused_computation.108 | convolution fusion | flops 1093665792 | bytes 19415040 | tf_op jit(solution)/shard_map/sub | solution.py:66
  187.1 7.2 %fusion.15 = bf16[1024,2,2,128]{0,3,2,1:T(8,128)(2,1)S(1)} fusion(bf16[1024,2,128,1]{0,2,3,1:T(8,128)(2,1)} %bitcast.81, f32[2,2,1024,1024]{2,3,1,0:T(8,128)} %get-tuple-element.31, f32[2,2,1024]{2,1,0:T(2,128)S(1)} %get-tuple-element.30), kind=kOutput, calls=%fused_computation.31 | convolution fusion | flops 1082654720 | bytes 18366464 | tf_op jit(solution)/shard_map/kgqs,skd->qkgd/dot_general | solution.py:68
  194.4 2.0 copy.70
  196.4 1.5 reshape_reshape.4
  197.9 0.8 fusion.16
  198.7 1.5 copy.71
  200.3 5.6 %all-to-all-start.1 = ((bf16[16,64,512]{2,0,1:T(8,128)(2,1)}), bf16[16,64,512]{2,0,1:T(8,128)(2,1)}, u32[]{:S(2)}, u32[]{:S(2)}) async-start(bf16[16,64,512]{2,0,1:T(8,128)(2,1)} %copy.71), calls=%async_computation.1 | async-start | bytes 2097152 | tf_op jit(solution)/shard_map/all_to_all | solution.py:126
  205.9 0.0 all-gather.2.cloned.1.call-start
  206.0 0.8 scatter_custom_fusion
  206.7 0.1 convert_reduce_fusion
  206.8 0.1 select_reduce_fusion.1
  207.0 27.6 %all-to-all-done.1 = bf16[16,64,512]{2,0,1:T(8,128)(2,1)} async-done(((bf16[16,64,512]{2,0,1:T(8,128)(2,1)}), bf16[16,64,512]{2,0,1:T(8,128)(2,1)}, u32[]{:S(2)}, u32[]{:S(2)}) %all-to-all-start.1) | async-done | bytes 1048608 | tf_op jit(solution)/shard_map/all_to_all | solution.py:126
  234.6 1.8 copy.72
  236.5 1.2 gather_fusion.1
  237.6 0.8 broadcast_select_fusion
  238.4 0.0 all-gather.2.cloned.1.call-update
  238.5 1.1 maximum_convert_fusion
  239.5 1.1 maximum_bitcast_fusion
  240.7 1.3 copy.73
  242.0 20.0 %all-gather.2.cloned.1.call-done = bf16[256,2048]{1,0:T(8,128)(2,1)} async-done(((bf16[256,512]{1,0:T(8,128)(2,1)}), bf16[256,2048]{1,0:T(8,128)(2,1)}) %all-gather.2.cloned.1.call-update) | async-done | bytes 1048592 | tf_op jit(solution)/shard_map/all_gather | solution.py:130
  261.9 1.9 convolution_convert_fusion.1
  263.9 1.7 add_convert_fusion.1
  (35 shorter events, 0.2 us)
Async XLA Ops:
  7.2 254.8 %copy-start = (bf16[2048,512]{1,0:T(8,128)(2,1)S(1)}, bf16[2048,512]{1,0:T(8,128)(2,1)}, u32[]{:S(2)}) copy-start(bf16[2048,512]{1,0:T(8,128)(2,1)} %param.19) | copy-start | bytes 6291460
  30.9 15.6 %copy-start.8 = (bf16[2048]{0:T(1024)(128)(2,1)S(1)}, bf16[2048]{0:T(1024)(128)(2,1)}, u32[]{:S(2)}) copy-start(bf16[2048]{0:T(1024)(128)(2,1)} %param.13) | copy-start | bytes 12292
  30.9 108.4 %all-to-all-start = ((bf16[16,64,2048]{2,0,1:T(8,128)(2,1)}), bf16[16,64,2048]{2,0,1:T(8,128)(2,1)}, u32[]{:S(2)}, u32[]{:S(2)}) async-start(bf16[16,64,2048]{2,0,1:T(8,128)(2,1)} %fusion.10), calls=%async_computation | async-start | bytes 8388608 | tf_op jit(solution)/shard_map/all_to_all | solution.py:112
  43.2 7.2 %copy-start.10 = (bf16[128]{0:T(256)(128)(2,1)S(1)}, bf16[128]{0:T(256)(128)(2,1)}, u32[]{:S(2)}) copy-start(bf16[128]{0:T(256)(128)(2,1)} %param.17) | copy-start | bytes 772
  43.2 7.2 %copy-start.6 = (bf16[2048,256]{1,0:T(8,128)(2,1)S(1)}, bf16[2048,256]{1,0:T(8,128)(2,1)}, u32[]{:S(2)}) copy-start(bf16[2048,256]{1,0:T(8,128)(2,1)} %param.15) | copy-start | bytes 3145732
  43.2 8.6 %copy-start.11 = (bf16[128]{0:T(256)(128)(2,1)S(1)}, bf16[128]{0:T(256)(128)(2,1)}, u32[]{:S(2)}) copy-start(bf16[128]{0:T(256)(128)(2,1)} %param.18) | copy-start | bytes 772
  150.3 5.8 %copy-start.1 = (f32[16,64,2048]{2,1,0:T(8,128)S(1)}, f32[16,64,2048]{2,1,0:T(8,128)}, u32[]{:S(2)}) copy-start(f32[16,64,2048]{2,1,0:T(8,128)} %get-tuple-element.17) | copy-start | bytes 25165828
  156.1 3.4 %copy-start.3 = (bf16[16,64,2048]{2,1,0:T(8,128)(2,1)}, bf16[16,64,2048]{2,1,0:T(8,128)(2,1)S(1)}, u32[]{:S(2)}) copy-start(bf16[16,64,2048]{2,1,0:T(8,128)(2,1)S(1)} %multiply_convert_fusion) | copy-start | bytes 12582916
  156.1 3.4 %copy-start.4 = (bf16[512,2048]{1,0:T(8,128)(2,1)S(1)}, bf16[512,2048]{1,0:T(8,128)(2,1)}, u32[]{:S(2)}) copy-start(bf16[512,2048]{1,0:T(8,128)(2,1)} %copy.80) | copy-start | bytes 6291460
  167.4 5.0 %copy-start.9 = (bf16[2048,256]{1,0:T(8,128)(2,1)S(1)}, bf16[2048,256]{1,0:T(8,128)(2,1)}, u32[]{:S(2)}) copy-start(bf16[2048,256]{1,0:T(8,128)(2,1)} %param.16) | copy-start | bytes 3145732
  171.3 2.3 copy-start.2
  173.6 2.1 copy-start.7
  173.6 2.1 copy-start.5
  200.3 34.4 %all-to-all-start.1 = ((bf16[16,64,512]{2,0,1:T(8,128)(2,1)}), bf16[16,64,512]{2,0,1:T(8,128)(2,1)}, u32[]{:S(2)}, u32[]{:S(2)}) async-start(bf16[16,64,512]{2,0,1:T(8,128)(2,1)} %copy.71), calls=%async_computation.1 | async-start | bytes 2097152 | tf_op jit(solution)/shard_map/all_to_all | solution.py:126
  205.9 56.0 %all-gather.2.cloned.1.call-start = ((), (), s32[]{:S(2)}) async-start(), calls=%async_computation.2 | async-start | bytes 1310720 | tf_op jit(solution)/shard_map/all_gather | solution.py:130
Sparse Core Ops, SparseCore 0:
  238.6 23.3 all-gather.1
where the time goes:
time: 273 us; the launch traced here: 272 us
  waiting for transfers between devices  132 us (48%)
  local copies, waits for them, and re-layouts  39.9 us (15%)
  other arithmetic  37.2 us (14%)
  matrix products  29 us (11%)
  starting transfers between devices  18 us (7%)
  between operations  16.3 us (6%)
    all_to_all x1, waiting for transfers between devices, on_device(): lax.all_to_all(jnp.where(send_valid[:, :, None], picked, jnp.zeros((), hi...  84.4 us
    all_to_all x1, waiting for transfers between devices, on_device(): lax.all_to_all(sendback, 'req', split_axis=1, concat_axis=1, tiled=True)  27.6 us
    all_gather x1, waiting for transfers between devices, on_device(): lax.all_gather(attended, 'tp', axis=1, tiled=True)  20 us
    all_to_all x1, starting transfers between devices, on_device(): lax.all_to_all(jnp.where(send_valid[:, :, None], picked, jnp.zeros((), hi...  12.3 us
    sub x1, matrix products, attend(): weights = jnp.exp(scores - row_max)  11.5 us
    gather x1, local copies, waits for them, and re-layouts, on_device(): jnp.take(hidden, send_rows, axis=0)  10.2 us
    select_n x1, other arithmetic, on_device(): jnp.where(send_valid[:, :, None], picked, jnp.zeros((), hidden.dtype))  9.61 us
    dot_general x1, matrix products, attend(): jnp.einsum('kgqs,skd->qkgd', weights, values_split, preferred_element_typ...  7.24 us
  transfers between devices with their start and end apart: 3, of which 3 were waited for; matrix products, arithmetic and copies ran while one was open for 5% of the time, Pallas kernels for 0%

commit v1 on v0

--- a/solution.py
+++ b/solution.py
@@ -5,6 +5,28 @@
 
 EPS = 1e-06
 THETA = 1000000.0
+
+
+def in_order(blocks, dim):
+    lengths = list(blocks.shape[1:])
+    lengths[dim] *= blocks.shape[0]
+    return jnp.moveaxis(blocks, 0, dim).reshape(lengths)
+
+
+def collect(value, axis, dim):
+    peers = lax.axis_size(axis)
+    pairs = [(i, (i + 1) % peers) for i in range(peers)]
+    back = [(b, a) for a, b in pairs]
+    lower, upper = ([], [])
+    for lap in range(peers - 1):
+        if lap % 2 == 0:
+            lower.append(lax.ppermute(lower[-1] if lower else value, axis, pairs))
+        else:
+            upper.append(lax.ppermute(upper[-1] if upper else value, axis, back))
+    parts = jnp.stack([*lower[::-1], value, *upper])
+    shift = lax.axis_index(axis) - len(lower)
+    parts = parts[(jnp.arange(peers) - shift) % peers]
+    return in_order(parts, dim)
 
 
 def rms_rows(values, scale_gain):
@@ -126,11 +148,7 @@
     returned = lax.all_to_all(sendback, "req", split_axis=1, concat_axis=1, tiled=True)
     attended = jnp.take(returned.reshape(capacity * devices, -1), back_rows, axis=0)
     kv_cache = jnp.stack([key_slot, value_slot])[:, None]
-    summed = jnp.dot(
-        lax.all_gather(attended, "tp", axis=1, tiled=True),
-        w_out,
-        preferred_element_type=jnp.float32,
-    )
+    summed = jnp.dot(collect(attended, "tp", 1), w_out, preferred_element_type=jnp.float32)
     branch = lax.optimization_barrier(summed.astype(jnp.bfloat16))
     residual = lax.dynamic_slice_in_dim(hidden, slice_index * out_width, out_width, 1)
     hidden_out = (residual.astype(jnp.float32) + branch.astype(jnp.float32)).astype(jnp.bfloat16)

time: 273 us -> 257 us (0.941)
  between operations: 16.3 us -> 2.94 us
  waiting for transfers between devices: 132 us -> 121 us
  starting transfers between devices: 18 us -> 21.6 us
  local copies, waits for them, and re-layouts: 39.9 us -> 42.9 us
    all_gather x1 -> x0, waiting for transfers between devices: 20 us -> none  [on_device(): lax.all_gather(attended, 'tp', axis=1, tiled=True)]
    ppermute x0 -> x3, waiting for transfers between devices: none -> 9.28 us  [the longest x2 9.28 us: collect(): lower.append(lax.ppermute(lower[-1] if lower else value, axis, pairs))]
    ppermute x0 -> x3, starting transfers between devices: none -> 3.62 us  [the longest x2 1.88 us: collect(): lower.append(lax.ppermute(lower[-1] if lower else value, axis, pairs))]
  transfers between devices with their start and end apart: 3 -> 5, of which waited for: 3 -> 4; matrix products, arithmetic and copies ran while one was open for 5% -> 6% of each run, Pallas kernels for 0% -> 0%
where the time goes in v1:
time: 257 us; the launch traced here: 255 us
  waiting for transfers between devices  121 us (47%)
  local copies, waits for them, and re-layouts  42.9 us (17%)
  other arithmetic  38.6 us (15%)
  matrix products  27.8 us (11%)
  starting transfers between devices  21.6 us (8%)
  between operations  2.94 us (1%)
    all_to_all x1, waiting for transfers between devices, on_device(): lax.all_to_all(jnp.where(send_valid[:, :, None], picked, jnp.zeros((), hi...  84.4 us
    all_to_all x1, waiting for transfers between devices, on_device(): lax.all_to_all(sendback, 'req', split_axis=1, concat_axis=1, tiled=True)  27.7 us
    all_to_all x1, starting transfers between devices, on_device(): lax.all_to_all(jnp.where(send_valid[:, :, None], picked, jnp.zeros((), hi...  12.3 us
    sub x1, matrix products, attend(): weights = jnp.exp(scores - row_max)  11.5 us
    gather x1, local copies, waits for them, and re-layouts, on_device(): jnp.take(hidden, send_rows, axis=0)  10.2 us
    select_n x1, other arithmetic, on_device(): jnp.where(send_valid[:, :, None], picked, jnp.zeros((), hidden.dtype))  9.61 us
    ppermute x2, waiting for transfers between devices, collect(): lower.append(lax.ppermute(lower[-1] if lower else value, axis, pairs))  9.28 us
    dot_general x1, matrix products, attend(): jnp.einsum('kgqs,skd->qkgd', weights, values_split, preferred_element_typ...  7.24 us
  transfers between devices with their start and end apart: 5, of which 4 were waited for; matrix products, arithmetic and copies ran while one was open for 6% of the time, Pallas kernels for 0%

profile of v1, /device:TPU:2, one launch (start us, length us, event | category | flops | bytes accessed | tf_op | source)
XLA Modules:
  0.0 255.2 jit_solution(5002934812355951578)
XLA Ops:
  0.7 0.9 copy.61
  1.6 0.1 reduce-window.8
  1.6 0.1 reduce.1
  1.8 0.7 sub.101
  2.4 0.8 select_reduce_fusion.2
  3.3 0.7 compare_select_fusion.8
  4.0 0.1 compare_and_fusion
  4.2 0.1 copy.62
  4.4 0.1 copy.63
  4.5 10.2 %gather_fusion = bf16[1024,2048]{1,0:T(8,128)(2,1)} fusion(bf16[256,2048]{1,0:T(8,128)(2,1)} %param.10, s32[1024]{0:T(1024)S(1)} %broadcast_clamp_fusion), kind=kCustom, calls=%fused_computation | custom fusion | bytes 8392704 | tf_op jit(solution)/shard_map/jit(_take)/gather | solution.py:133
  14.7 9.6 %fusion.10 = bf16[16,64,2048]{2,0,1:T(8,128)(2,1)} fusion(bf16[16,64,2048]{2,1,0:T(8,128)(2,1)} %bitcast.79, pred[16,64]{0,1:T(8,128)(4,1)S(1)} %copy.63, pred[16,64]{0,1:T(8,128)(4,1)S(1)} %copy.62), kind=kLoop, calls=%fused_computation.23 | loop fusion | flops 4194304 | bytes 8390656 | tf_op jit(solution)/shard_map/jit(_where)/select_n | solution.py:135
  24.3 12.3 %all-to-all-start = ((bf16[16,64,2048]{2,0,1:T(8,128)(2,1)}), bf16[16,64,2048]{2,0,1:T(8,128)(2,1)}, u32[]{:S(2)}, u32[]{:S(2)}) async-start(bf16[16,64,2048]{2,0,1:T(8,128)(2,1)} %fusion.10), calls=%async_computation | async-start | bytes 8388608 | tf_op jit(solution)/shard_map/all_to_all | solution.py:134
  36.7 0.6 dynamic_slice.19
  39.3 0.6 dynamic_slice.21
  39.9 4.0 %copy.84 = bf16[512,2048]{1,0:T(8,128)(2,1)} copy(bf16[512,2048]{0,1:T(8,128)(2,1)} %bitcast.86) | data formatting | bytes 4194304 | tf_op jit(solution)/shard_map/dot_general | solution.py:58
  43.9 1.4 copy.81
  45.3 0.7 iota_compare_fusion.3
  46.0 1.0 multiply_cosine_fusion
  47.0 1.3 fusion.11
  48.3 84.4 %all-to-all-done = bf16[16,64,2048]{2,0,1:T(8,128)(2,1)} async-done(((bf16[16,64,2048]{2,0,1:T(8,128)(2,1)}), bf16[16,64,2048]{2,0,1:T(8,128)(2,1)}, u32[]{:S(2)}, u32[]{:S(2)}) %all-to-all-start) | async-done | bytes 4194336 | tf_op jit(solution)/shard_map/all_to_all | solution.py:134
  132.8 4.5 %copy.65 = bf16[16,64,2048]{2,1,0:T(8,128)(2,1)S(1)} copy(bf16[16,64,2048]{2,0,1:T(8,128)(2,1)} %all-to-all-done) | data formatting | bytes 8388608 | tf_op jit(solution)/shard_map/all_to_all | solution.py:134
  137.3 6.5 %multiply_reduce_fusion = (f32[16,64]{1,0:T(8,128)S(1)}, f32[16,64,2048]{2,1,0:T(8,128)}) fusion(s32[]{:T(128)S(6)} %select_n.198, bf16[16,64,2048]{2,1,0:T(8,128)(2,1)S(1)} %copy.65), kind=kLoop, calls=%fused_computation.17 | loop fusion | flops 12581888 | bytes 12587012 | tf_op jit(solution)/shard_map/reduce_sum | solution.py:33
  143.8 4.3 %multiply_convert_fusion = bf16[16,64,2048]{2,1,0:T(8,128)(2,1)S(1)} fusion(f32[16,64,2048]{2,1,0:T(8,128)} %get-tuple-element.17, f32[2048]{0:T(1024)S(1)} %convert_element_type.122, f32[16,64]{1,0:T(8,128)S(1)} %add_rsqrt_fusion.2), kind=kLoop, calls=%fused_computation.16 | loop fusion | flops 6291456 | bytes 12595200 | tf_op jit(solution)/shard_map/convert_element_type | solution.py:142
  148.1 1.5 copy-done.1
  149.6 2.7 %fusion.3 = bf16[1024,2048]{1,0:T(8,128)(2,1)} fusion(f32[16,64,2048]{2,1,0:T(8,128)S(1)} %copy-done.1, f32[2048]{0:T(1024)S(1)} %convert_element_type.122, f32[1024]{0:T(1024)S(1)} %rsqrt.29), kind=kLoop, calls=%fused_computation.13 | loop fusion | flops 6291456 | bytes 12595200 | tf_op jit(solution)/shard_map/convert_element_type | solution.py:142
  152.3 0.7 copy-done.3
  153.0 2.4 multiply_reduce_fusion.1
  155.4 0.5 multiply_multiply_fusion
  155.9 1.2 subtract_convert_fusion
  157.1 2.4 copy.70
  159.5 1.4 copy.69
  160.9 3.9 %multiply_reduce_fusion.2 = (f32[1024,2]{0,1:T(2,128)S(1)}, f32[1024,2,128]{0,2,1:T(8,128)S(1)}) fusion(bf16[1024,2048,1]{1,0,2:T(8,128)(2,1)} %bitcast.83, bf16[2,128,2048]{2,1,0:T(8,128)(2,1)} %bitcast.90), kind=kOutput, calls=%fused_computation.43 | convolution fusion | flops 1074264064 | bytes 6299648 | tf_op jit(solution)/shard_map/dot_general | solution.py:61
  164.8 0.2 multiply_multiply_fusion.1
  165.0 0.9 multiply_subtract_fusion
  165.9 1.2 copy-done.2
  167.0 2.1 convolution_convert_fusion
  169.1 11.5 %fusion.40 = (f32[2,2,1024]{2,1,0:T(2,128)S(1)}, f32[2,2,1024,1024]{2,3,1,0:T(8,128)}) fusion(pred[1024,1024]{0,1:T(8,128)(4,1)S(1)} %copy-done.5, bf16[1024,2,2,64]{3,0,2,1:T(8,128)(2,1)} %copy.70, bf16[1024,2,2,64]{3,0,2,1:T(8,128)(2,1)} %copy.69, bf16[1024,2,64]{0,2,1:T(8,128)(2,1)} %get-tuple-element.21, bf16[1024,2,64]{0,2,1:T(8,128)(2,1)S(1)} %get-tuple-element.20), kind=kOutput, calls=%fused_computation.118 | convolution fusion | flops 1093665792 | bytes 19415040 | tf_op jit(solution)/shard_map/sub | solution.py:88
  180.6 7.2 %fusion.15 = bf16[1024,2,2,128]{0,3,2,1:T(8,128)(2,1)S(1)} fusion(bf16[1024,2,128,1]{0,2,3,1:T(8,128)(2,1)} %bitcast.92, f32[2,2,1024,1024]{2,3,1,0:T(8,128)} %get-tuple-element.31, f32[2,2,1024]{2,1,0:T(2,128)S(1)} %get-tuple-element.30), kind=kOutput, calls=%fused_computation.32 | convolution fusion | flops 1082654720 | bytes 18366464 | tf_op jit(solution)/shard_map/kgqs,skd->qkgd/dot_general | solution.py:90
  187.9 2.0 copy.73
  189.9 1.5 reshape_reshape.4
  191.4 0.8 fusion.16
  192.2 1.5 copy.74
  193.7 5.6 %all-to-all-start.1 = ((bf16[16,64,512]{2,0,1:T(8,128)(2,1)}), bf16[16,64,512]{2,0,1:T(8,128)(2,1)}, u32[]{:S(2)}, u32[]{:S(2)}) async-start(bf16[16,64,512]{2,0,1:T(8,128)(2,1)} %copy.74), calls=%async_computation.1 | async-start | bytes 2097152 | tf_op jit(solution)/shard_map/all_to_all | solution.py:148
  199.4 0.8 scatter_custom_fusion
  200.2 0.1 convert_reduce_fusion
  200.3 0.1 select_reduce_fusion.1
  200.4 27.7 %all-to-all-done.1 = bf16[16,64,512]{2,0,1:T(8,128)(2,1)} async-done(((bf16[16,64,512]{2,0,1:T(8,128)(2,1)}), bf16[16,64,512]{2,0,1:T(8,128)(2,1)}, u32[]{:S(2)}, u32[]{:S(2)}) %all-to-all-start.1) | async-done | bytes 1048608 | tf_op jit(solution)/shard_map/all_to_all | solution.py:148
  228.1 1.8 copy.75
  229.9 1.2 gather_fusion.1
  231.1 0.8 broadcast_select_fusion
  231.9 1.6 collective-permute-start
  233.5 1.1 maximum_convert_fusion
  234.5 1.7 collective-permute-start.2
  236.3 4.3 %collective-permute-done = bf16[256,512]{1,0:T(8,128)(2,1)} collective-permute-done((bf16[256,512]{1,0:T(8,128)(2,1)}, bf16[256,512]{1,0:T(8,128)(2,1)}, u32[]{:S(2)}, u32[]{:S(2)}) %collective-permute-start) | collective-permute-done | bytes 262176 | tf_op jit(solution)/shard_map/ppermute | solution.py:23
  240.5 0.3 collective-permute-start.1
  240.8 1.1 maximum_bitcast_fusion
  242.0 1.3 copy.77
  243.3 0.1 bitcast_select_fusion.4
  243.4 5.0 %collective-permute-done.1 = bf16[256,512]{1,0:T(8,128)(2,1)} collective-permute-done((bf16[256,512]{1,0:T(8,128)(2,1)}, bf16[256,512]{1,0:T(8,128)(2,1)}, u32[]{:S(2)}, u32[]{:S(2)}) %collective-permute-start.1) | collective-permute-done | bytes 262176 | tf_op jit(solution)/shard_map/ppermute | solution.py:23
  248.4 1.2 pad_maximum_fusion.1
  249.7 1.6 gather_fusion.2
  251.3 1.5 copy.76
  252.8 0.7 convolution_convert_fusion.1
  253.5 1.7 add_convert_fusion.1
  (44 shorter events, 0.5 us)
Async XLA Ops:
  0.6 252.1 %copy-start = (bf16[2048,512]{1,0:T(8,128)(2,1)S(1)}, bf16[2048,512]{1,0:T(8,128)(2,1)}, u32[]{:S(2)}) copy-start(bf16[2048,512]{1,0:T(8,128)(2,1)} %param.19) | copy-start | bytes 6291460
  24.3 15.6 %copy-start.8 = (bf16[2048]{0:T(1024)(128)(2,1)S(1)}, bf16[2048]{0:T(1024)(128)(2,1)}, u32[]{:S(2)}) copy-start(bf16[2048]{0:T(1024)(128)(2,1)} %param.13) | copy-start | bytes 12292
  24.3 108.4 %all-to-all-start = ((bf16[16,64,2048]{2,0,1:T(8,128)(2,1)}), bf16[16,64,2048]{2,0,1:T(8,128)(2,1)}, u32[]{:S(2)}, u32[]{:S(2)}) async-start(bf16[16,64,2048]{2,0,1:T(8,128)(2,1)} %fusion.10), calls=%async_computation | async-start | bytes 8388608 | tf_op jit(solution)/shard_map/all_to_all | solution.py:134
  36.7 7.2 %copy-start.10 = (bf16[128]{0:T(256)(128)(2,1)S(1)}, bf16[128]{0:T(256)(128)(2,1)}, u32[]{:S(2)}) copy-start(bf16[128]{0:T(256)(128)(2,1)} %param.17) | copy-start | bytes 772
  36.7 7.2 %copy-start.6 = (bf16[2048,256]{1,0:T(8,128)(2,1)S(1)}, bf16[2048,256]{1,0:T(8,128)(2,1)}, u32[]{:S(2)}) copy-start(bf16[2048,256]{1,0:T(8,128)(2,1)} %param.15) | copy-start | bytes 3145732
  36.7 8.6 %copy-start.11 = (bf16[128]{0:T(256)(128)(2,1)S(1)}, bf16[128]{0:T(256)(128)(2,1)}, u32[]{:S(2)}) copy-start(bf16[128]{0:T(256)(128)(2,1)} %param.18) | copy-start | bytes 772
  143.8 5.8 %copy-start.1 = (f32[16,64,2048]{2,1,0:T(8,128)S(1)}, f32[16,64,2048]{2,1,0:T(8,128)}, u32[]{:S(2)}) copy-start(f32[16,64,2048]{2,1,0:T(8,128)} %get-tuple-element.17) | copy-start | bytes 25165828
  149.6 3.4 %copy-start.3 = (bf16[16,64,2048]{2,1,0:T(8,128)(2,1)}, bf16[16,64,2048]{2,1,0:T(8,128)(2,1)S(1)}, u32[]{:S(2)}) copy-start(bf16[16,64,2048]{2,1,0:T(8,128)(2,1)S(1)} %multiply_convert_fusion) | copy-start | bytes 12582916
  149.6 3.4 %copy-start.4 = (bf16[512,2048]{1,0:T(8,128)(2,1)S(1)}, bf16[512,2048]{1,0:T(8,128)(2,1)}, u32[]{:S(2)}) copy-start(bf16[512,2048]{1,0:T(8,128)(2,1)} %copy.84) | copy-start | bytes 6291460
  160.9 5.0 %copy-start.9 = (bf16[2048,256]{1,0:T(8,128)(2,1)S(1)}, bf16[2048,256]{1,0:T(8,128)(2,1)}, u32[]{:S(2)}) copy-start(bf16[2048,256]{1,0:T(8,128)(2,1)} %param.16) | copy-start | bytes 3145732
  164.8 2.3 copy-start.2
  167.0 2.1 copy-start.7
  167.0 2.1 copy-start.5
  193.7 34.4 %all-to-all-start.1 = ((bf16[16,64,512]{2,0,1:T(8,128)(2,1)}), bf16[16,64,512]{2,0,1:T(8,128)(2,1)}, u32[]{:S(2)}, u32[]{:S(2)}) async-start(bf16[16,64,512]{2,0,1:T(8,128)(2,1)} %copy.74), calls=%async_computation.1 | async-start | bytes 2097152 | tf_op jit(solution)/shard_map/all_to_all | solution.py:148
  231.9 8.7 %collective-permute-start = (bf16[256,512]{1,0:T(8,128)(2,1)}, bf16[256,512]{1,0:T(8,128)(2,1)}, u32[]{:S(2)}, u32[]{:S(2)}) collective-permute-start(bf16[256,512]{1,0:T(8,128)(2,1)} %broadcast_select_fusion), channel_id=1, source_target_pairs={{0,1},{1,2},{2,3},{3,0},{4,5},{5,6},{6,7},{7,4},{8,9},{9,10},{10,1... | collective-permute-start | bytes 786440 | tf_op jit(solution)/shard_map/ppermute | solution.py:23
  234.5 8.9 %collective-permute-start.2 = (bf16[256,512]{1,0:T(8,128)(2,1)}, bf16[256,512]{1,0:T(8,128)(2,1)}, u32[]{:S(2)}, u32[]{:S(2)}) collective-permute-start(bf16[256,512]{1,0:T(8,128)(2,1)} %broadcast_select_fusion), channel_id=1, source_target_pairs={{1,0},{2,1},{3,2},{0,3},{5,4},{6,5},{7,6},{4,7},{9,8},{10,9},{11,1... | collective-permute-start | bytes 786440 | tf_op jit(solution)/shard_map/ppermute | solution.py:25
  240.5 7.9 %collective-permute-start.1 = (bf16[256,512]{1,0:T(8,128)(2,1)}, bf16[256,512]{1,0:T(8,128)(2,1)}, u32[]{:S(2)}, u32[]{:S(2)}) collective-permute-start(bf16[256,512]{1,0:T(8,128)(2,1)} %collective-permute-done), channel_id=1, source_target_pairs={{0,1},{1,2},{2,3},{3,0},{4,5},{5,6},{6,7},{7,4},{8,9},{9,10},{10,1... | collective-permute-start | bytes 786440 | tf_op jit(solution)/shard_map/ppermute | solution.py:23
